TPU v7x, 256 devices: a whole 4x4x8 slice. The times are simulated.
256 devices in a mesh: dp: 32 (over x, z_hi, y), mp: 8 (over z_lo, core).
Axes of the slice: x: 4, y: 4, z: 8 (z_hi: 2, z_lo: 4; z = z_hi * 4 + z_lo), core: 2. Of those that a mesh axis runs over, the one named last changes fastest.
Arguments:
- store_rows: bfloat16 [8192, 8192], P('dp', 'mp'), may hold values from -6 to 6
- source_shard: int32 [1024], replicated, may hold values from 0 to 31, as said below
- source_row: int32 [1024], replicated, may hold values from 0 to 255
- state_len: int32 [32], replicated, may hold values from 1 to 64, 1024 in all
- visits: int32 [32], replicated, may hold values from 1 to 4095
- gain: bfloat16 [8192], P('mp'), may hold values from 0.5 to 1.5
- w_gate: bfloat16 [8192, 22016], P('mp', 'dp'), may hold values from -0.0625 to 0.0625
- w_up: bfloat16 [8192, 22016], P('mp', 'dp'), may hold values from -0.0625 to 0.0625
- w_down: bfloat16 [22016, 8192], P('dp', 'mp'), may hold values from -0.0390625 to 0.0390625
- upstream: bfloat16 [1024, 8192], P(None, 'mp'), may hold values from -0.375 to 0.375
Outputs:
- layer_out: bfloat16 [1024, 8192], P('dp', 'mp')
- grad_gate: bfloat16 [8192, 22016], P('mp', 'dp')
- grad_up: bfloat16 [8192, 22016], P('mp', 'dp')
- grad_down: bfloat16 [22016, 8192], P('dp', 'mp')
Inputs may be any that keep to these rules, and one draw needn't show every extreme that they name: `source_shard`: block b holds training rows b * 32 to (b + 1) * 32 - 1. No shard is named more than 4 times in one block nor more than 128 times in all; one shard, drawn from the seed, is named exactly 4 times in every block. `state_len`: the lengths sum to 1024.
All inputs are finite; a program needn't handle non-finite values.
Results may differ from a plain program's by a relative error of at most 0.017.
Values may be sent and summed in bfloat16 or wider, within the bound.
No kernel may reach another device: no remote copies, remote signals or barrier semaphores. Data moves between devices by JAX's collectives and lax.ppermute only.
A program may use at most 64 MiB of HBM per device.

v0:
```python
import jax
import jax.numpy as jnp
from jax import lax
from jax.sharding import Mesh
from jax.sharding import PartitionSpec as P

D = 8192
epsilon = 1e-05
DP = ("x", "zh", "y")
MP = ("zl", "c")


def shards(
    store_rows, source_shard, source_row, state_len, visits, gain, w_gate, w_up, w_down, upstream
):
    f32, bf16 = (jnp.float32, jnp.bfloat16)
    count_dp = 1
    for name in DP:
        count_dp *= lax.axis_size(name)
    index_dp = lax.axis_index(DP)
    total_rows = source_shard.shape[0]
    block_rows = total_rows // count_dp
    pair_cap = max(block_rows // 8, 1)
    store_dev = store_rows.shape[0]
    hidden_dev = w_gate.shape[1]
    shard = source_shard.reshape(count_dp, block_rows)
    srow = source_row.reshape(count_dp, block_rows)
    same = shard[:, :, None] == shard[:, None, :]
    t_ids = jnp.arange(block_rows, dtype=jnp.int32)
    earlier = t_ids[None, :] < t_ids[:, None]
    rank = jnp.sum((same & earlier[None]).astype(jnp.int32), axis=2)
    owned = shard == index_dp
    slots = jnp.arange(pair_cap, dtype=jnp.int32)
    hit = owned[:, :, None] & (rank[:, :, None] == slots[None, None, :])
    slot_row = jnp.sum(jnp.where(hit, srow[:, :, None] + 1, 0), axis=1) - 1
    pick_out = (
        slot_row.reshape(count_dp * pair_cap)[:, None]
        == jnp.arange(store_dev, dtype=jnp.int32)[None, :]
    ).astype(bf16)
    outgoing = jnp.dot(pick_out, store_rows, preferred_element_type=f32).astype(bf16)
    received = lax.all_to_all(outgoing, DP, 0, 0, tiled=True)
    my_shard = lax.dynamic_index_in_dim(shard, index_dp, 0, keepdims=False)
    my_rank = lax.dynamic_index_in_dim(rank, index_dp, 0, keepdims=False)
    pick_in = (
        (my_shard * pair_cap + my_rank)[:, None]
        == jnp.arange(count_dp * pair_cap, dtype=jnp.int32)[None, :]
    ).astype(bf16)
    own_rows = jnp.dot(pick_in, received, preferred_element_type=f32).astype(bf16)
    train_rows = own_rows
    for name in reversed(DP):
        train_rows = lax.all_gather(train_rows, name, axis=0, tiled=True)
    rows_float = train_rows.astype(f32)
    squares = jnp.sum(rows_float * rows_float, axis=1)
    scaled = (rows_float * gain.astype(f32)[None, :]).astype(bf16)
    gate_term = jnp.dot(scaled, w_gate, preferred_element_type=f32)
    up_term = jnp.dot(scaled, w_up, preferred_element_type=f32)
    packed = jnp.concatenate([gate_term, up_term, squares[:, None]], axis=1)
    total = lax.psum(packed, MP)
    gate_total = total[:, :hidden_dev]
    up_total = total[:, hidden_dev : 2 * hidden_dev]
    square_total = total[:, 2 * hidden_dev]
    inverse = lax.rsqrt(square_total / D + epsilon)
    gate_all = inverse[:, None] * gate_total
    up_all = inverse[:, None] * up_total
    hidden_all = (jax.nn.silu(gate_all) * up_all).astype(bf16)
    down_part = jnp.dot(hidden_all, w_down, preferred_element_type=f32).astype(bf16)
    down_in = lax.all_to_all(down_part, DP, 0, 0, tiled=True)
    down_block = jnp.sum(
        down_in.reshape(count_dp, block_rows, down_in.shape[1]).astype(f32), axis=0
    )
    layer_out = (own_rows.astype(f32) + down_block).astype(bf16)
    row_ids = jnp.arange(total_rows, dtype=jnp.int32)
    ends = jnp.cumsum(state_len)
    starts = ends - state_len
    member = ((row_ids[:, None] >= starts[None, :]) & (row_ids[:, None] < ends[None, :])).astype(
        f32
    )
    importance = jnp.log1p(visits.astype(f32))
    per_state = total_rows * importance / (state_len.astype(f32) * jnp.sum(importance))
    row_weight = jnp.sum(member * per_state[None, :], axis=1)
    out_grad = (upstream.astype(f32) * row_weight[:, None]).astype(bf16)
    grad_down = lax.dot_general(
        hidden_all, out_grad, (((0,), (0,)), ((), ())), preferred_element_type=f32
    ).astype(bf16)
    hidden_term = lax.dot_general(
        out_grad, w_down, (((1,), (1,)), ((), ())), preferred_element_type=f32
    ).astype(bf16)
    grad_hidden = lax.psum(hidden_term, MP).astype(f32)
    sigmoid_gate = jax.nn.sigmoid(gate_all)
    gate_delta = (
        inverse[:, None]
        * grad_hidden
        * up_all
        * sigmoid_gate
        * (1.0 + gate_all * (1.0 - sigmoid_gate))
    ).astype(bf16)
    up_delta = (inverse[:, None] * grad_hidden * gate_all * sigmoid_gate).astype(bf16)
    grad_gate = lax.dot_general(
        scaled, gate_delta, (((0,), (0,)), ((), ())), preferred_element_type=f32
    ).astype(bf16)
    grad_up = lax.dot_general(
        scaled, up_delta, (((0,), (0,)), ((), ())), preferred_element_type=f32
    ).astype(bf16)
    return (layer_out, grad_gate, grad_up, grad_down)


def solution(mesh):
    sizes = dict(zip(mesh.axis_names, mesh.devices.shape))
    count_mp = sizes["mp"]
    count_dp = sizes["dp"]
    zh = 2
    y = 4
    x = count_dp // (zh * y)
    c = 2
    zl = count_mp // c
    view = Mesh(mesh.devices.reshape(x, zh, y, zl, c), DP + MP)
    in_specs = (P(DP, MP), P(), P(), P(), P(), P(MP), P(MP, DP), P(MP, DP), P(DP, MP), P(None, MP))
    out_specs = (P(DP, MP), P(MP, DP), P(MP, DP), P(DP, MP))
    return jax.shard_map(shards, mesh=view, in_specs=in_specs, out_specs=out_specs, check_vma=False)
```

profile of v0, /device:TPU:2, one launch (start us, length us, event | category | flops | bytes accessed | tf_op | source)
XLA Modules:
  0.0 380.9 jit_solution(1981180116354993840)
XLA Ops:
  7.2 0.9 reshape.93
  8.1 0.8 convert_reduce_fusion.1
  10.0 1.3 convolution_convert_fusion.5
  11.3 0.8 all_to_all.14
  12.1 14.2 %all-to-all-start = ((bf16[32,4,1024]{2,1,0:T(4,128)(2,1)}), bf16[32,4,1024]{2,1,0:T(4,128)(2,1)S(1)}, u32[]{:S(2)}, u32[]{:S(2)}) async-start(bf16[32,4,1024]{2,1,0:T(4,128)(2,1)} %all_to_all.14), calls=%async_computation | async-start | bytes 524288 | tf_op jit(solution)/shard_map/all_to_all | solution.py:41
  26.5 12.0 %all-to-all-done = bf16[32,4,1024]{2,1,0:T(4,128)(2,1)S(1)} async-done(((bf16[32,4,1024]{2,1,0:T(4,128)(2,1)}), bf16[32,4,1024]{2,1,0:T(4,128)(2,1)S(1)}, u32[]{:S(2)}, u32[]{:S(2)}) %all-to-all-start) | async-done | bytes 262176 | tf_op jit(solution)/shard_map/all_to_all | solution.py:41
  39.4 12.2 %all_gather.9 = bf16[128,1024]{1,0:T(8,128)(2,1)S(1)} all-gather(bf16[32,1024]{1,0:T(8,128)(2,1)S(1)} %convolution_convert_fusion.6), channel_id=1, replica_groups=mesh['x'=4,'zh'=2,'y'=4,'zl'=4,'c'=2] {'y'}, dimensions={0}, use_global_device_ids=true | all-gather | bytes 327680 | tf_op jit(solution)/shard_map/all_gather | solution.py:51
  51.6 13.8 %all_gather.10 = bf16[256,1024]{1,0:T(8,128)(2,1)} all-gather(bf16[128,1024]{1,0:T(8,128)(2,1)S(1)} %all_gather.9), channel_id=1, replica_groups=mesh['x'=4,'zh'=2,'y'=4,'zl'=4,'c'=2] {'zh'}, dimensions={0}, use_global_device_ids=true | all-gather | bytes 786432 | tf_op jit(solution)/shard_map/all_gather | solution.py:51
  65.5 28.7 %all-gather.2.cloned.1.call-done = bf16[1024,1024]{1,0:T(8,128)(2,1)} async-done(((bf16[256,1024]{1,0:T(8,128)(2,1)}), bf16[1024,1024]{1,0:T(8,128)(2,1)}) %all-gather.2.cloned.1.call-update) | async-done | bytes 2097168 | tf_op jit(solution)/shard_map/all_gather | solution.py:51
  94.3 2.1 fusion.1
  96.4 3.4 fusion.4
  99.8 1.7 fusion.6
  101.5 3.0 pad_maximum_fusion
  105.4 137.3 %all-reduce.3.cloned.1.call-done = f32[1024,1377]{0,1:T(8,128)} async-done(((f32[1024,1377]{0,1:T(8,128)}), f32[1024,1377]{0,1:T(8,128)}) %all-reduce.3.cloned.1.call-update) | async-done | bytes 5640208 | tf_op jit(solution)/shard_map/psum | solution.py:58
  242.8 0.8 fusion.13
  243.5 3.5 multiply_convert_fusion.3
  247.0 3.2 convolution_convert_fusion
  250.2 10.0 %all-to-all-start.1 = ((bf16[32,32,1024]{2,1,0:T(8,128)(2,1)}), bf16[32,32,1024]{2,1,0:T(8,128)(2,1)S(1)}, u32[]{:S(2)}, u32[]{:S(2)}) async-start(bf16[32,32,1024]{2,1,0:T(8,128)(2,1)} %bitcast.14), calls=%async_computation.1 | async-start | bytes 4194304 | tf_op jit(solution)/shard_map/all_to_all | solution.py:67
  261.9 4.4 %convolution_convert_fusion.4 = bf16[1024,688]{0,1:T(8,128)(2,1)} fusion(bf16[688,1024]{1,0:T(8,128)(2,1)S(1)} %copy-done, bf16[1024,1024]{1,0:T(8,128)(2,1)} %param.19, f32[1024]{0:T(1024)S(1)} %select_reduce_fusion), kind=kOutput, calls=%fused_computation.18 | convolution fusion | flops 1446690816 | bytes 4919296 | tf_op jit(solution)/shard_map/dot_general | solution.py:85
  266.3 4.8 %convolution_convert_fusion.3 = bf16[688,1024]{1,0:T(8,128)(2,1)} fusion(bf16[1024,688]{0,1:T(8,128)(2,1)} %copy-done.3, bf16[1024,1024]{1,0:T(8,128)(2,1)} %param.19, f32[1024]{0:T(1024)S(1)} %select_reduce_fusion), kind=kOutput, calls=%fused_computation.17 | convolution fusion | flops 1446690816 | bytes 4919296 | tf_op jit(solution)/shard_map/dot_general | solution.py:82
  271.1 89.1 %all-reduce.5.cloned.1.call-done = bf16[1024,688]{0,1:T(8,128)(2,1)} async-done(((bf16[1024,688]{0,1:T(8,128)(2,1)}), bf16[1024,688]{0,1:T(8,128)(2,1)}) %all-reduce.5.cloned.1.call-update) | async-done | bytes 1409040 | tf_op jit(solution)/shard_map/psum | solution.py:88
  360.2 6.1 %convolution_convert_fusion.1 = bf16[1024,688]{0,1:T(8,128)(2,1)} fusion(bf16[1024,688]{0,1:T(8,128)(2,1)} %all-reduce.5.cloned.1.call-done, f32[1024,1377]{0,1:T(8,128)} %all-reduce.3.cloned.1.call-done, f32[1024]{0:T(1024)S(1)} %bitcast.17, bf16[1024,1024]{1,0:T(8,128)(2,1)} %all-gather.2.cloned.1.call-done, f32[1024]{0:T(1024)S(1)} %convert_element_type.74), kind=kOutput, calls=%fused_computation.15 | convolution fusion | flops 1453031424 | bytes 7741440 | tf_op jit(solution)/shard_map/dot_general | solution.py:101
  366.3 6.3 %convolution_convert_fusion.2 = bf16[1024,688]{0,1:T(8,128)(2,1)} fusion(bf16[1024,688]{0,1:T(8,128)(2,1)S(1)} %copy-done.10, f32[1024,1377]{0,1:T(8,128)} %all-reduce.3.cloned.1.call-done, f32[1024]{0:T(1024)S(1)} %bitcast.18, bf16[1024,1024]{1,0:T(8,128)(2,1)S(1)} %copy-done.2, f32[1024]{0:T(1024)S(1)} %convert_element_type.74), kind=kOutput, calls=%fused_computation.16 | convolution fusion | flops 1456553984 | bytes 10559488 | tf_op jit(solution)/shard_map/dot_general | solution.py:98
  372.9 1.5 add_convert_fusion
  (49 shorter events, 5.1 us)
Async XLA Ops:
  7.2 239.8 %copy-start = (bf16[688,1024]{1,0:T(8,128)(2,1)S(1)}, bf16[688,1024]{1,0:T(8,128)(2,1)}, u32[]{:S(2)}) copy-start(bf16[688,1024]{1,0:T(8,128)(2,1)} %param.18) | copy-start | bytes 4227076
  7.2 58.3 %copy-start.5 = (bf16[1024]{0:T(1024)(128)(2,1)S(1)}, bf16[1024]{0:T(1024)(128)(2,1)}, u32[]{:S(2)}) copy-start(bf16[1024]{0:T(1024)(128)(2,1)} %param.15) | copy-start | bytes 6148
  11.3 85.0 %copy-start.8 = (bf16[1024,688]{0,1:T(8,128)(2,1)S(1)}, bf16[1024,688]{0,1:T(8,128)(2,1)}, u32[]{:S(2)}) copy-start(bf16[1024,688]{0,1:T(8,128)(2,1)} %param.17) | copy-start | bytes 4227076
  12.1 26.3 %all-to-all-start = ((bf16[32,4,1024]{2,1,0:T(4,128)(2,1)}), bf16[32,4,1024]{2,1,0:T(4,128)(2,1)S(1)}, u32[]{:S(2)}, u32[]{:S(2)}) async-start(bf16[32,4,1024]{2,1,0:T(4,128)(2,1)} %all_to_all.14), calls=%async_computation | async-start | bytes 524288 | tf_op jit(solution)/shard_map/all_to_all | solution.py:41
  26.4 67.9 %all-gather.2.cloned.1.call-start = ((), (), s32[]{:S(2)}) async-start(), calls=%async_computation.2 | async-start | bytes 2621440 | tf_op jit(solution)/shard_map/all_gather | solution.py:51
  38.7 0.6 copy-start.4
  65.5 177.3 %all-reduce.3.cloned.1.call-start = ((), (), s32[]{:S(2)}) async-start(), calls=%async_computation.3 | async-start | bytes 11337728 | tf_op jit(solution)/shard_map/psum | solution.py:58
  96.4 3.4 copy-start.1
  96.4 3.4 copy-start.9
  104.5 0.7 copy-start.6
  247.0 3.2 copy-start.3
  250.2 10.3 %copy-start.7 = (s32[32]{0:T(128)S(1)}, s32[32]{0:T(128)}, u32[]{:S(2)}) copy-start(s32[32]{0:T(128)} %param.14) | copy-start | bytes 388
  250.2 122.4 %all-to-all-start.1 = ((bf16[32,32,1024]{2,1,0:T(8,128)(2,1)}), bf16[32,32,1024]{2,1,0:T(8,128)(2,1)S(1)}, u32[]{:S(2)}, u32[]{:S(2)}) async-start(bf16[32,32,1024]{2,1,0:T(8,128)(2,1)} %bitcast.14), calls=%async_computation.1 | async-start | bytes 4194304 | tf_op jit(solution)/shard_map/all_to_all | solution.py:67
  260.2 100.0 %all-reduce.5.cloned.1.call-start = ((), (), s32[]{:S(2)}) async-start(), calls=%async_computation.4 | async-start | bytes 2818048 | tf_op jit(solution)/shard_map/psum | solution.py:88
  360.2 6.1 %copy-start.2 = (bf16[1024,1024]{1,0:T(8,128)(2,1)S(1)}, bf16[1024,1024]{1,0:T(8,128)(2,1)}, u32[]{:S(2)}) copy-start(bf16[1024,1024]{1,0:T(8,128)(2,1)} %all-gather.2.cloned.1.call-done) | copy-start | bytes 6291460
  360.2 6.1 %copy-start.10 = (bf16[1024,688]{0,1:T(8,128)(2,1)S(1)}, bf16[1024,688]{0,1:T(8,128)(2,1)}, u32[]{:S(2)}) copy-start(bf16[1024,688]{0,1:T(8,128)(2,1)} %all-reduce.5.cloned.1.call-done) | copy-start | bytes 4227076
Sparse Core Ops, SparseCore 0:
  65.6 28.6 all-gather.1
  104.6 138.0 all-reduce.2
  266.4 93.7 all-reduce.4
where the time goes:
time: 382 us; the launch traced here: 381 us
  waiting for transfers between devices  267 us (70%)
  matrix products  31.4 us (8%)
  blocking collectives  26.1 us (7%)
  starting transfers between devices  24.6 us (6%)
  other arithmetic  14.4 us (4%)
  between operations  14 us (4%)
    psum x1, waiting for transfers between devices, shards(): total = lax.psum(packed, MP)  137 us
    psum x1, waiting for transfers between devices, shards(): grad_hidden = lax.psum(hidden_term, MP).astype(f32)  89.1 us
    all_gather x1, waiting for transfers between devices, shards(): train_rows = lax.all_gather(train_rows, name, axis=0, tiled=True)  28.7 us
    all_gather x2, blocking collectives, shards(): train_rows = lax.all_gather(train_rows, name, axis=0, tiled=True)  26.1 us
    all_to_all x1, starting transfers between devices, shards(): received = lax.all_to_all(outgoing, DP, 0, 0, tiled=True)  14.2 us
    all_to_all x1, waiting for transfers between devices, shards(): received = lax.all_to_all(outgoing, DP, 0, 0, tiled=True)  12 us
    all_to_all x1, starting transfers between devices, shards(): down_in = lax.all_to_all(down_part, DP, 0, 0, tiled=True)  10 us
  transfers between devices with their start and end apart: 5, of which 4 were waited for; matrix products, arithmetic and copies ran while one was open for 6% of the time, Pallas kernels for 0%

commit v1 on v0

--- a/solution.py
+++ b/solution.py
@@ -48,7 +48,9 @@
     own_rows = jnp.dot(pick_in, received, preferred_element_type=f32).astype(bf16)
     train_rows = own_rows
     for name in reversed(DP):
-        train_rows = lax.all_gather(train_rows, name, axis=0, tiled=True)
+        train_rows = jnp.concatenate(
+            lax.all_to_all(jnp.stack([train_rows] * lax.axis_size(name)), name, 0, 0), axis=0
+        )
     rows_float = train_rows.astype(f32)
     squares = jnp.sum(rows_float * rows_float, axis=1)
     scaled = (rows_float * gain.astype(f32)[None, :]).astype(bf16)

time: 382 us -> 377 us (0.987)
  waiting for transfers between devices: 267 us -> 257 us
  starting transfers between devices: 24.6 us -> 29.6 us
    all_gather x1 -> x0, waiting for transfers between devices: 28.7 us -> none  [shards(): train_rows = lax.all_gather(train_rows, name, axis=0, tiled=True)]
    all_to_all x0 -> x2, blocking collectives: none -> 26.9 us  [shards(): lax.all_to_all(jnp.stack([train_rows] * lax.axis_size(name)), name, 0, 0)]
    all_gather x2 -> x0, blocking collectives: 26.1 us -> none  [shards(): train_rows = lax.all_gather(train_rows, name, axis=0, tiled=True)]
    all_to_all x0 -> x1, waiting for transfers between devices: none -> 17.4 us  [shards(): lax.all_to_all(jnp.stack([train_rows] * lax.axis_size(name)), name, 0, 0)]
    all_to_all x0 -> x1, starting transfers between devices: none -> 5.11 us  [shards(): lax.all_to_all(jnp.stack([train_rows] * lax.axis_size(name)), name, 0, 0)]
where the time goes in v1:
time: 377 us; the launch traced here: 376 us
  waiting for transfers between devices  257 us (68%)
  starting transfers between devices  29.6 us (8%)
  matrix products  29.3 us (8%)
  blocking collectives  26.9 us (7%)
  between operations  14.2 us (4%)
  other arithmetic  13.4 us (4%)
  local copies, waits for them, and re-layouts  5.04 us (1%)
    psum x1, waiting for transfers between devices, shards(): total = lax.psum(packed, MP)  139 us
    psum x1, waiting for transfers between devices, shards(): grad_hidden = lax.psum(hidden_term, MP).astype(f32)  88.9 us
    all_to_all x2, blocking collectives, shards(): lax.all_to_all(jnp.stack([train_rows] * lax.axis_size(name)), name, 0, 0)  26.9 us
    all_to_all x1, waiting for transfers between devices, shards(): lax.all_to_all(jnp.stack([train_rows] * lax.axis_size(name)), name, 0, 0)  17.4 us
    all_to_all x1, starting transfers between devices, shards(): received = lax.all_to_all(outgoing, DP, 0, 0, tiled=True)  14.2 us
    all_to_all x1, waiting for transfers between devices, shards(): received = lax.all_to_all(outgoing, DP, 0, 0, tiled=True)  12 us
    all_to_all x1, starting transfers between devices, shards(): down_in = lax.all_to_all(down_part, DP, 0, 0, tiled=True)  10 us
  transfers between devices with their start and end apart: 5, of which 4 were waited for; matrix products, arithmetic and copies ran while one was open for 6% of the time, Pallas kernels for 0%

profile of v1, /device:TPU:2, one launch (start us, length us, event | category | flops | bytes accessed | tf_op | source)
XLA Modules:
  0.0 375.8 jit_solution(3873781843032737663)
XLA Ops:
  7.2 0.9 reshape.102
  10.0 1.3 convolution_convert_fusion.5
  11.3 0.8 all_to_all.23
  12.1 14.2 %all-to-all-start = ((bf16[32,4,1024]{2,1,0:T(4,128)(2,1)}), bf16[32,4,1024]{2,1,0:T(4,128)(2,1)S(1)}, u32[]{:S(2)}, u32[]{:S(2)}) async-start(bf16[32,4,1024]{2,1,0:T(4,128)(2,1)} %all_to_all.23), calls=%async_computation | async-start | bytes 524288 | tf_op jit(solution)/shard_map/all_to_all | solution.py:41
  26.4 12.0 %all-to-all-done = bf16[32,4,1024]{2,1,0:T(4,128)(2,1)S(1)} async-done(((bf16[32,4,1024]{2,1,0:T(4,128)(2,1)}), bf16[32,4,1024]{2,1,0:T(4,128)(2,1)S(1)}, u32[]{:S(2)}, u32[]{:S(2)}) %all-to-all-start) | async-done | bytes 262176 | tf_op jit(solution)/shard_map/all_to_all | solution.py:41
  38.7 9.1 %all_to_all.36 = bf16[4,32,1024]{2,1,0:T(8,128)(2,1)S(1)} all-to-all(bf16[4,32,1024]{2,1,0:T(8,128)(2,1)S(1)} %stack.6), channel_id=1, replica_groups=mesh['x'=4,'zh'=2,'y'=4,'zl'=4,'c'=2] {'y'}, dimensions={0} | all-to-all | bytes 524288 | tf_op jit(solution)/shard_map/all_to_all | solution.py:52
  47.9 17.8 %all_to_all.37 = bf16[2,128,1024]{2,1,0:T(8,128)(2,1)S(1)} all-to-all(bf16[2,128,1024]{2,1,0:T(8,128)(2,1)S(1)} %pad_maximum_fusion.1), channel_id=1, replica_groups=mesh['x'=4,'zh'=2,'y'=4,'zl'=4,'c'=2] {'zh'}, dimensions={0} | all-to-all | bytes 1048576 | tf_op jit(solution)/shard_map/all_to_all | solution.py:52
  65.7 1.6 stack.15
  67.3 5.1 %all-to-all-start.3 = ((bf16[4,256,1024]{2,1,0:T(8,128)(2,1)}), bf16[4,256,1024]{2,1,0:T(8,128)(2,1)S(1)}, u32[]{:S(2)}, u32[]{:S(2)}) async-start(bf16[4,256,1024]{2,1,0:T(8,128)(2,1)} %stack.15), calls=%async_computation.3 | async-start | bytes 4194304 | tf_op jit(solution)/shard_map/all_to_all | solution.py:52
  72.4 17.4 %all-to-all-done.3 = bf16[4,256,1024]{2,1,0:T(8,128)(2,1)S(1)} async-done(((bf16[4,256,1024]{2,1,0:T(8,128)(2,1)}), bf16[4,256,1024]{2,1,0:T(8,128)(2,1)S(1)}, u32[]{:S(2)}, u32[]{:S(2)}) %all-to-all-start.3) | async-done | bytes 2097184 | tf_op jit(solution)/shard_map/all_to_all | solution.py:52
  90.4 0.8 copy-done.8
  91.2 1.7 fusion.10
  93.3 1.7 fusion.11
  95.5 3.0 pad_maximum_fusion
  98.5 139.0 %all-reduce.3.cloned.1.call-done = f32[1024,1377]{0,1:T(8,128)} async-done(((f32[1024,1377]{0,1:T(8,128)}), f32[1024,1377]{0,1:T(8,128)}) %all-reduce.3.cloned.1.call-update) | async-done | bytes 5640208 | tf_op jit(solution)/shard_map/psum | solution.py:60
  238.3 3.5 multiply_convert_fusion.3
  241.8 3.2 convolution_convert_fusion
  245.0 10.0 %all-to-all-start.4 = ((bf16[32,32,1024]{2,1,0:T(8,128)(2,1)}), bf16[32,32,1024]{2,1,0:T(8,128)(2,1)S(1)}, u32[]{:S(2)}, u32[]{:S(2)}) async-start(bf16[32,32,1024]{2,1,0:T(8,128)(2,1)} %bitcast.28), calls=%async_computation.4 | async-start | bytes 4194304 | tf_op jit(solution)/shard_map/all_to_all | solution.py:69
  256.9 4.4 %convolution_convert_fusion.4 = bf16[1024,688]{0,1:T(8,128)(2,1)} fusion(bf16[688,1024]{1,0:T(8,128)(2,1)S(1)} %copy-done, bf16[1024,1024]{1,0:T(8,128)(2,1)} %param.19, f32[1024]{0:T(1024)S(1)} %select_reduce_fusion), kind=kOutput, calls=%fused_computation.17 | convolution fusion | flops 1446690816 | bytes 4919296 | tf_op jit(solution)/shard_map/dot_general | solution.py:87
  261.3 4.8 %convolution_convert_fusion.3 = bf16[688,1024]{1,0:T(8,128)(2,1)} fusion(bf16[1024,688]{0,1:T(8,128)(2,1)} %copy-done.3, bf16[1024,1024]{1,0:T(8,128)(2,1)} %param.19, f32[1024]{0:T(1024)S(1)} %select_reduce_fusion), kind=kOutput, calls=%fused_computation.16 | convolution fusion | flops 1446690816 | bytes 4919296 | tf_op jit(solution)/shard_map/dot_general | solution.py:84
  266.2 88.9 %all-reduce.5.cloned.1.call-done = bf16[1024,688]{0,1:T(8,128)(2,1)} async-done(((bf16[1024,688]{0,1:T(8,128)(2,1)}), bf16[1024,688]{0,1:T(8,128)(2,1)}) %all-reduce.5.cloned.1.call-update) | async-done | bytes 1409040 | tf_op jit(solution)/shard_map/psum | solution.py:90
  355.0 5.9 %convolution_convert_fusion.1 = bf16[1024,688]{0,1:T(8,128)(2,1)} fusion(bf16[1024,1024]{1,0:T(8,128)(2,1)} %copy-done.1, bf16[1024,688]{0,1:T(8,128)(2,1)} %all-reduce.5.cloned.1.call-done, f32[1024,1377]{0,1:T(8,128)} %all-reduce.3.cloned.1.call-done, f32[1024]{0:T(1024)S(1)} %bitcast.32), kind=kOutput, calls=%fused_computation.14 | convolution fusion | flops 1449885696 | bytes 7737344 | tf_op jit(solution)/shard_map/dot_general | solution.py:103
  361.0 6.1 %convolution_convert_fusion.2 = bf16[1024,688]{0,1:T(8,128)(2,1)} fusion(bf16[1024,1024]{1,0:T(8,128)(2,1)S(1)} %copy-done.2, bf16[1024,688]{0,1:T(8,128)(2,1)S(1)} %copy-done.10, f32[1024,1377]{0,1:T(8,128)} %all-reduce.3.cloned.1.call-done, f32[1024]{0:T(1024)S(1)} %bitcast.33), kind=kOutput, calls=%fused_computation.15 | convolution fusion | flops 1453408256 | bytes 10555392 | tf_op jit(solution)/shard_map/dot_general | solution.py:100
  367.4 1.5 add_convert_fusion
  (53 shorter events, 6.8 us)
Async XLA Ops:
  7.2 234.6 %copy-start = (bf16[688,1024]{1,0:T(8,128)(2,1)S(1)}, bf16[688,1024]{1,0:T(8,128)(2,1)}, u32[]{:S(2)}) copy-start(bf16[688,1024]{1,0:T(8,128)(2,1)} %param.18) | copy-start | bytes 4227076
  12.1 26.3 %all-to-all-start = ((bf16[32,4,1024]{2,1,0:T(4,128)(2,1)}), bf16[32,4,1024]{2,1,0:T(4,128)(2,1)S(1)}, u32[]{:S(2)}, u32[]{:S(2)}) async-start(bf16[32,4,1024]{2,1,0:T(4,128)(2,1)} %all_to_all.23), calls=%async_computation | async-start | bytes 524288 | tf_op jit(solution)/shard_map/all_to_all | solution.py:41
  38.7 9.1 %copy-start.4 = (bf16[32,1024]{1,0:T(8,128)(2,1)}, bf16[32,1024]{1,0:T(8,128)(2,1)S(1)}, u32[]{:S(2)}) copy-start(bf16[32,1024]{1,0:T(8,128)(2,1)S(1)} %convolution_convert_fusion.6) | copy-start | bytes 196612
  65.7 6.8 %copy-start.5 = (bf16[1024]{0:T(1024)(128)(2,1)S(1)}, bf16[1024]{0:T(1024)(128)(2,1)}, u32[]{:S(2)}) copy-start(bf16[1024]{0:T(1024)(128)(2,1)} %param.15) | copy-start | bytes 6148
  67.3 22.5 %all-to-all-start.3 = ((bf16[4,256,1024]{2,1,0:T(8,128)(2,1)}), bf16[4,256,1024]{2,1,0:T(8,128)(2,1)S(1)}, u32[]{:S(2)}, u32[]{:S(2)}) async-start(bf16[4,256,1024]{2,1,0:T(8,128)(2,1)} %stack.15), calls=%async_computation.3 | async-start | bytes 4194304 | tf_op jit(solution)/shard_map/all_to_all | solution.py:52
  72.4 165.1 %all-reduce.3.cloned.1.call-start = ((), (), s32[]{:S(2)}) async-start(), calls=%async_computation.5 | async-start | bytes 11337728 | tf_op jit(solution)/shard_map/psum | solution.py:60
  89.8 1.4 copy-start.8
  91.2 1.7 copy-start.1
  91.2 2.1 copy-start.9
  241.8 3.2 copy-start.3
  245.0 10.3 %copy-start.6 = (s32[32]{0:T(128)S(1)}, s32[32]{0:T(128)}, u32[]{:S(2)}) copy-start(s32[32]{0:T(128)} %param.13) | copy-start | bytes 388
  245.0 10.5 %copy-start.7 = (s32[32]{0:T(128)S(1)}, s32[32]{0:T(128)}, u32[]{:S(2)}) copy-start(s32[32]{0:T(128)} %param.14) | copy-start | bytes 388
  245.0 122.1 %all-to-all-start.4 = ((bf16[32,32,1024]{2,1,0:T(8,128)(2,1)}), bf16[32,32,1024]{2,1,0:T(8,128)(2,1)S(1)}, u32[]{:S(2)}, u32[]{:S(2)}) async-start(bf16[32,32,1024]{2,1,0:T(8,128)(2,1)} %bitcast.28), calls=%async_computation.4 | async-start | bytes 4194304 | tf_op jit(solution)/shard_map/all_to_all | solution.py:69
  255.0 100.0 %all-reduce.5.cloned.1.call-start = ((), (), s32[]{:S(2)}) async-start(), calls=%async_computation.6 | async-start | bytes 2818048 | tf_op jit(solution)/shard_map/psum | solution.py:90
  355.0 5.9 %copy-start.2 = (bf16[1024,1024]{1,0:T(8,128)(2,1)S(1)}, bf16[1024,1024]{1,0:T(8,128)(2,1)}, u32[]{:S(2)}) copy-start(bf16[1024,1024]{1,0:T(8,128)(2,1)} %copy-done.1) | copy-start | bytes 6291460
  355.0 5.9 %copy-start.10 = (bf16[1024,688]{0,1:T(8,128)(2,1)S(1)}, bf16[1024,688]{0,1:T(8,128)(2,1)}, u32[]{:S(2)}) copy-start(bf16[1024,688]{0,1:T(8,128)(2,1)} %all-reduce.5.cloned.1.call-done) | copy-start | bytes 4227076
Sparse Core Ops, SparseCore 0:
  98.7 138.8 all-reduce.2
  261.5 93.5 all-reduce.4
